TPU v7x, 32 devices: a whole 2x2x4 slice. The times are simulated.
32 devices in a mesh: clips: 2 (over y), space: 8 (over z, x), tm: 2 (over core).
Axes of the slice: x: 2, y: 2, z: 4, core: 2. Of those that a mesh axis runs over, the one named last changes fastest.
Arguments:
- frames: bfloat16 [2, 2, 16, 112, 192], P('clips', 'tm', 'space'), parts along dimension 0, may hold values from -100 to 100
- norm1_gain: float32 [192], replicated, may hold values from 0.1 to 1.9
- conv1_weight: bfloat16 [3, 3, 3, 192, 192], replicated, may hold values from -0.078125 to 0.078125
- conv1_bias: float32 [192], replicated, may hold values from -3 to 3
- norm2_gain: float32 [192], replicated, may hold values from 0.1 to 1.9
- conv2_weight: bfloat16 [3, 3, 3, 192, 192], replicated, may hold values from -0.078125 to 0.078125
- conv2_bias: float32 [192], replicated, may hold values from -3 to 3
- attn_gain: float32 [192], replicated, may hold values from 0.5 to 3
- w_query: bfloat16 [192, 192], replicated, may hold values from -3 to 3
- b_query: float32 [192], replicated, may hold values from -4 to 4
- w_key: bfloat16 [192, 192], replicated, may hold values from -1 to 2
- w_value: bfloat16 [192, 192], replicated, may hold values from -0.4375 to 0.4375
- b_value: float32 [192], replicated, may hold values from -3 to 3
- w_out: bfloat16 [192, 192], replicated, may hold values from -0.4375 to 0.4375
- b_out: float32 [192], replicated, may hold values from -3 to 3
Outputs:
- decoded: float32 [2, 2, 16, 112, 192], P('clips', 'tm', 'space'), parts along dimension 0
There are 2 independent parts, one for each index of `clips`. A program takes and returns all parts, laid end to end along the dimension named above; an argument that names none is the same for every part. Nothing has to cross between parts.
All inputs are finite; a program needn't handle non-finite values.
Results may differ from a plain program's by a relative error of at most 0.02.
Values may be sent and summed in bfloat16 or wider, within the bound.
No kernel may reach another device: no remote copies, remote signals or barrier semaphores. Data moves between devices by JAX's collectives and lax.ppermute only.
A program may use at most 128 MiB of HBM per device.

v0:
```python
import math
import jax
import jax.numpy as jnp
from jax import lax
from jax.sharding import PartitionSpec as P

epsilon = 1e-06


def shifted(block, axis, distance):
    devices = range(lax.axis_size(axis))
    route = [((i - distance) % len(devices), i) for i in devices]
    return lax.ppermute(block, axis, route)


def extended(value, sides, width):
    for axis, dim in sides:
        size, length = (lax.axis_size(axis), value.shape[dim])
        up = [(i, (i + 1) % size) for i in range(size - 1)]
        down = [(j, i) for i, j in up]
        last = lax.slice_in_dim(value, length - width, length, axis=dim)
        first = lax.slice_in_dim(value, 0, width, axis=dim)
        before = lax.ppermute(last, axis, up)
        after = lax.ppermute(first, axis, down)
        value = jnp.concatenate([before, value, after], axis=dim)
    return value


def rms_scale(values, gain):
    return values * lax.rsqrt(jnp.mean(values * values, axis=-1, keepdims=True) + epsilon) * gain


def causal_conv(inputs, weight, bias):
    frame_count, row_count, col_count, channels = inputs.shape
    is_first = lax.axis_index("tm") == 0
    remote = shifted(inputs, "tm", 1)
    earlier = jnp.concatenate([jnp.zeros_like(remote), remote[:-1]], axis=0)
    previous = jnp.where(is_first, earlier, remote)
    paired = extended(jnp.stack([inputs, previous]), (("space", 2),), 1)
    current = paired[0]
    previous = paired[1]
    oldest = jnp.concatenate([jnp.zeros_like(current), current[:-1]], axis=0)
    tap_list = []
    for source in (oldest, previous, current):
        widened = jnp.pad(source, ((0, 0), (0, 0), (1, 1), (0, 0)))
        for row_off in range(3):
            for col_off in range(3):
                tap_list.append(
                    widened[:, row_off : row_off + row_count, col_off : col_off + col_count, :]
                )
    patches = jnp.concatenate(tap_list, axis=-1).reshape(
        frame_count * row_count * col_count, 27 * channels
    )
    summed = jnp.dot(
        patches, weight.reshape(27 * channels, channels), preferred_element_type=jnp.float32
    )
    return summed.reshape(frame_count, row_count, col_count, channels) + bias


def absorb(running, queries, key_rows):
    top_old, total_old, accum = running
    scores = jnp.einsum("fqc,fkc->fqk", queries, key_rows, preferred_element_type=jnp.float32)
    top_new = jnp.maximum(top_old, jnp.max(scores, axis=-1))
    weights = jnp.exp(scores - top_new[..., None])
    total_new = jnp.sum(weights, axis=-1)
    accum = jnp.einsum(
        "fqk,fkc->fqc", weights.astype(jnp.bfloat16), key_rows, preferred_element_type=jnp.float32
    )
    return (top_new, total_new, accum)


def local(
    frames,
    norm1_gain,
    conv1_weight,
    conv1_bias,
    norm2_gain,
    conv2_weight,
    conv2_bias,
    attn_gain,
    w_query,
    b_query,
    w_key,
    w_value,
    b_value,
    w_out,
    b_out,
):
    local_frames = frames[:, 0]
    frame_count, row_count, col_count, channels = local_frames.shape
    frame_values = local_frames.astype(jnp.float32)
    first_act = jax.nn.silu(rms_scale(frame_values, norm1_gain)).astype(jnp.bfloat16)
    first_out = causal_conv(first_act, conv1_weight, conv1_bias)
    second_act = jax.nn.silu(rms_scale(first_out, norm2_gain)).astype(jnp.bfloat16)
    second_out = causal_conv(second_act, conv2_weight, conv2_bias)
    residual = frame_values + second_out
    normed = rms_scale(residual, attn_gain).astype(jnp.bfloat16)
    token_count = row_count * col_count
    flat = normed.reshape(frame_count * token_count, channels)
    query = (jnp.dot(flat, w_query, preferred_element_type=jnp.float32) + b_query).astype(
        jnp.bfloat16
    )
    folded = (
        jnp.dot(query, w_key.T, preferred_element_type=jnp.float32) * (1.0 / math.sqrt(channels))
    ).astype(jnp.bfloat16)
    folded = folded.reshape(frame_count, token_count, channels)
    initial = (
        jnp.full((frame_count, token_count), -1e30, jnp.float32),
        jnp.zeros((frame_count, token_count), jnp.float32),
        jnp.zeros((frame_count, token_count, channels), jnp.float32),
    )
    slot_queries = folded

    def absorb_one(running, received, offset, slot_queries=slot_queries):
        return absorb(running, slot_queries, received.reshape(1, -1, channels))

    start_state = tuple((item for item in initial))
    results = [
        absorb_one(
            start_state, lax.all_gather(normed[0], "space", axis=0, tiled=True), jnp.int32(0)
        )
    ]
    total = jnp.concatenate([item[1] for item in results], axis=0)
    accum = jnp.concatenate([item[2] for item in results], axis=0)
    mixed = (accum / total[..., None]).astype(jnp.bfloat16).reshape(-1, channels)
    value = (jnp.dot(mixed, w_value, preferred_element_type=jnp.float32) + b_value).astype(
        jnp.bfloat16
    )
    decoded = (
        residual.reshape(-1, channels)
        + jnp.dot(value, w_out, preferred_element_type=jnp.float32)
        + b_out
    )
    return decoded.reshape(frame_count, 1, row_count, col_count, channels)


def solution(mesh):
    placed = (
        P("clips", "tm", "space", None, None),
        P(),
        P(),
        P(),
        P(),
        P(),
        P(),
        P(),
        P(),
        P(),
        P(),
        P(),
        P(),
        P(),
        P(),
    )
    return jax.shard_map(
        local,
        mesh=mesh,
        in_specs=placed,
        out_specs=P("clips", "tm", "space", None, None),
        check_vma=False,
    )
```

profile of v0, /device:TPU:0, one launch (start us, length us, event | category | flops | bytes accessed | tf_op | source)
XLA Modules:
  0.0 90.7 jit_solution(12605600663512206442)
XLA Ops:
  0.0 1.1 %copy.31 = bf16[1,1,2,112,192]{4,3,2,1,0:T(8,128)(2,1)S(1)} copy(bf16[1,1,2,112,192]{3,4,2,1,0:T(8,128)(2,1)} %param.15) | data formatting | bytes 172032 | tf_op args[0]
  1.3 0.8 fusion.31
  3.7 4.8 %collective-permute-start.1 = (bf16[2,1,1,112,192]{4,3,2,1,0:T(8,128)(2,1)S(1)}, bf16[2,1,1,112,192]{4,3,2,1,0:T(8,128)(2,1)S(1)}, u32[]{:S(2)}, u32[]{:S(2)}) collective-permute-start(bf16[2,1,1,112,192]{4,3,2,1,0:T(8,128)(2,1)S(1)} %get-tuple-element.47), channel_id=1, source_target_pairs={{0,2},{2,4},{4,6},{6,8},{8,10},{10,12},{12,14},{1,3},{3,5},{5,7},{... | collective-permute-start | bytes 258056 | tf_op jit(solution)/shard_map/ppermute | solution.py:23
  8.4 1.3 %collective-permute-start.2 = (bf16[2,1,1,112,192]{4,3,2,1,0:T(8,128)(2,1)S(1)}, bf16[2,1,1,112,192]{4,3,2,1,0:T(8,128)(2,1)S(1)}, u32[]{:S(2)}, u32[]{:S(2)}) collective-permute-start(bf16[2,1,1,112,192]{4,3,2,1,0:T(8,128)(2,1)S(1)} %get-tuple-element.48), channel_id=1, source_target_pairs={{2,0},{4,2},{6,4},{8,6},{10,8},{12,10},{14,12},{3,1},{5,3},{7,5},{... | collective-permute-start | bytes 258056 | tf_op jit(solution)/shard_map/ppermute | solution.py:24
  9.8 1.3 %collective-permute-done.1 = bf16[2,1,1,112,192]{4,3,2,1,0:T(8,128)(2,1)S(1)} collective-permute-done((bf16[2,1,1,112,192]{4,3,2,1,0:T(8,128)(2,1)S(1)}, bf16[2,1,1,112,192]{4,3,2,1,0:T(8,128)(2,1)S(1)}, u32[]{:S(2)}, u32[]{:S(2)}) %collective-permute-start.1) | collective-permute-done | bytes 86048 | tf_op jit(solution)/shard_map/ppermute | solution.py:23
  11.1 4.1 %collective-permute-done.2 = bf16[2,1,1,112,192]{4,3,2,1,0:T(8,128)(2,1)S(1)} collective-permute-done((bf16[2,1,1,112,192]{4,3,2,1,0:T(8,128)(2,1)S(1)}, bf16[2,1,1,112,192]{4,3,2,1,0:T(8,128)(2,1)S(1)}, u32[]{:S(2)}, u32[]{:S(2)}) %collective-permute-start.2) | collective-permute-done | bytes 86048 | tf_op jit(solution)/shard_map/ppermute | solution.py:24
  15.4 1.2 %pad_slice_fusion.16 = (bf16[1,2,112,192]{3,2,1,0:T(8,128)(2,1)S(1)}, bf16[1,2,112,192]{3,2,1,0:T(8,128)(2,1)S(1)}, bf16[1,2,112,192]{3,2,1,0:T(8,128)(2,1)S(1)}...) fusion(bf16[1,4,112,192]{3,2,1,0:T(8,128)(2,1)S(1)} %get-tuple-, ...), kind=kLoop, calls=%fused_computation.67 | loop fusion | bytes 2695168 | tf_op jit(solution)/shard_map/slice | solution.py:49
  16.8 5.4 %concatenate.13 = bf16[1,2,112,5184]{3,2,1,0:T(8,128)(2,1)} concatenate(bf16[1,2,112,192]{3,2,1,0:T(8,128)(2,1)S(1)} %pad.24, bf16[1,2,112,192]{3,2,1,0:T(8,128)(2,1)S(1)} %pad.25, bf16[1,2,112,192]{3,2,1,0:T(8,128)(2,1)S(1)} %pad.26, bf16[1,2,112,192]{3,2,1,0:T(8,128)(2,1)S(1)} %pad.24, bf16[1,2,112,192]{3,2,1,0:T(8,128)(2,1)S(1)} %pad.25, bf16[1,2,112,192]{3,2,1,0:T(8,128)(2,1)S(1)} %pad.26, ...), dimensions={3} | concatenate | bytes 4644864 | tf_op jit(solution)/shard_map/concatenate | solution.py:51
  22.3 2.5 %multiply_reduce_fusion.1 = (f32[2,112]{1,0:T(2,128)S(1)}, f32[2,112,192]{2,1,0:T(8,128)S(1)}) fusion(f32[192]{0:T(256)S(1)} %copy-done.7, bf16[5184,192,1]{1,0,2:T(8,128)(2,1)S(1)} %bitcast.83, bf16[1,2,112,5184]{3,2,1,0:T(8,128)(2,1)} %concatenate.13), kind=kOutput, calls=%fused_computation.54 | convolution fusion | flops 446035744 | bytes 4486784 | tf_op jit(solution)/shard_map/dot_general | solution.py:54
  25.2 1.2 %collective-permute-done.3 = bf16[1,2,112,192]{3,2,1,0:T(8,128)(2,1)S(1)} collective-permute-done((bf16[1,2,112,192]{3,2,1,0:T(8,128)(2,1)S(1)}, bf16[1,2,112,192]{3,2,1,0:T(8,128)(2,1)S(1)}, u32[]{:S(2)}, u32[]{:S(2)}) %collective-permute-start.3) | collective-permute-done | bytes 86048 | tf_op jit(solution)/shard_map/ppermute | solution.py:13
  26.4 4.4 %collective-permute-start.4 = (bf16[2,1,1,112,192]{4,3,2,1,0:T(8,128)(2,1)S(1)}, bf16[2,1,1,112,192]{4,3,2,1,0:T(8,128)(2,1)S(1)}, u32[]{:S(2)}, u32[]{:S(2)}) collective-permute-start(bf16[2,1,1,112,192]{4,3,2,1,0:T(8,128)(2,1)S(1)} %get-tuple-element.27), channel_id=1, source_target_pairs={{0,2},{2,4},{4,6},{6,8},{8,10},{10,12},{12,14},{1,3},{3,5},{5,7},{... | collective-permute-start | bytes 258056 | tf_op jit(solution)/shard_map/ppermute | solution.py:23
  30.8 1.3 %collective-permute-start.5 = (bf16[2,1,1,112,192]{4,3,2,1,0:T(8,128)(2,1)S(1)}, bf16[2,1,1,112,192]{4,3,2,1,0:T(8,128)(2,1)S(1)}, u32[]{:S(2)}, u32[]{:S(2)}) collective-permute-start(bf16[2,1,1,112,192]{4,3,2,1,0:T(8,128)(2,1)S(1)} %get-tuple-element.28), channel_id=1, source_target_pairs={{2,0},{4,2},{6,4},{8,6},{10,8},{12,10},{14,12},{3,1},{5,3},{7,5},{... | collective-permute-start | bytes 258056 | tf_op jit(solution)/shard_map/ppermute | solution.py:24
  32.1 1.4 %collective-permute-done.4 = bf16[2,1,1,112,192]{4,3,2,1,0:T(8,128)(2,1)S(1)} collective-permute-done((bf16[2,1,1,112,192]{4,3,2,1,0:T(8,128)(2,1)S(1)}, bf16[2,1,1,112,192]{4,3,2,1,0:T(8,128)(2,1)S(1)}, u32[]{:S(2)}, u32[]{:S(2)}) %collective-permute-start.4) | collective-permute-done | bytes 86048 | tf_op jit(solution)/shard_map/ppermute | solution.py:23
  33.5 4.1 %collective-permute-done.5 = bf16[2,1,1,112,192]{4,3,2,1,0:T(8,128)(2,1)S(1)} collective-permute-done((bf16[2,1,1,112,192]{4,3,2,1,0:T(8,128)(2,1)S(1)}, bf16[2,1,1,112,192]{4,3,2,1,0:T(8,128)(2,1)S(1)}, u32[]{:S(2)}, u32[]{:S(2)}) %collective-permute-start.5) | collective-permute-done | bytes 86048 | tf_op jit(solution)/shard_map/ppermute | solution.py:24
  37.8 0.9 %pad_slice_fusion.4 = (bf16[1,2,112,192]{3,2,1,0:T(8,128)(2,1)S(1)}, bf16[1,2,112,192]{3,2,1,0:T(8,128)(2,1)S(1)}, bf16[1,2,112,192]{3,2,1,0:T(8,128)(2,1)S(1)},...) fusion(bf16[1,4,112,192]{3,2,1,0:T(8,128)(2,1)S(1)} %get-tuple-, ...), kind=kLoop, calls=%fused_computation.55 | loop fusion | bytes 1347584 | tf_op jit(solution)/shard_map/slice | solution.py:49
  38.7 1.0 %pad_slice_fusion.10 = (bf16[1,2,112,192]{3,2,1,0:T(8,128)(2,1)}, bf16[1,2,112,192]{3,2,1,0:T(8,128)(2,1)}, bf16[1,2,112,192]{3,2,1,0:T(8,128)(2,1)}, bf16[1,2,1...) fusion(bf16[1,4,112,192]{3,2,1,0:T(8,128)(2,1)S(1)} %get-tuple-, ...), kind=kLoop, calls=%fused_computation.61 | loop fusion | bytes 1347584 | tf_op jit(solution)/shard_map/slice | solution.py:49
  39.7 5.4 %concatenate.15 = bf16[1,2,112,5184]{3,2,1,0:T(8,128)(2,1)} concatenate(bf16[1,2,112,192]{3,2,1,0:T(8,128)(2,1)S(1)} %pad.24, bf16[1,2,112,192]{3,2,1,0:T(8,128)(2,1)S(1)} %pad.25, bf16[1,2,112,192]{3,2,1,0:T(8,128)(2,1)S(1)} %pad.26, bf16[1,2,112,192]{3,2,1,0:T(8,128)(2,1)S(1)} %pad.24, bf16[1,2,112,192]{3,2,1,0:T(8,128)(2,1)S(1)} %pad.25, bf16[1,2,112,192]{3,2,1,0:T(8,128)(2,1)S(1)} %pad.26, ...), dimensions={3} | concatenate | bytes 4644864 | tf_op jit(solution)/shard_map/concatenate | solution.py:51
  45.1 3.3 %multiply_reduce_fusion = (f32[2,112]{1,0:T(2,128)S(1)}, f32[2,112,192]{2,1,0:T(8,128)S(1)}) fusion(f32[192]{0:T(256)S(1)} %copy-done.8, bf16[5184,192,1]{1,0,2:T(8,128)(2,1)} %bitcast.86, bf16[1,2,112,5184]{3,2,1,0:T(8,128)(2,1)} %concatenate.15, bf16[1,1,2,112,192]{4,3,2,1,0:T(8,128)(2,1)S(1)} %copy.31), kind=kOutput, calls=%fused_computation.52 | convolution fusion | flops 446121760 | bytes 4572800 | tf_op jit(solution)/shard_map/dot_general | solution.py:54
  49.5 32.1 %all_gather.3 = bf16[16,112,192]{1,2,0:T(8,128)(2,1)S(1)} all-gather(bf16[2,112,192]{1,2,0:T(8,128)(2,1)S(1)} %copy.36), channel_id=1, replica_groups=mesh['clips'=2,'space'=8,'tm'=2] {'space'}, dimensions={0}, use_global_device_ids=true | all-gather | bytes 774144 | tf_op jit(solution)/shard_map/all_gather | solution.py:120
  82.0 1.8 %reshape.197 = bf16[1792,192]{0,1:T(8,128)(2,1)} reshape(bf16[16,112,192]{1,0,2:T(8,128)(2,1)S(1)} %copy.37) | data formatting | bytes 1376256 | tf_op jit(solution)/shard_map/reshape.9
  83.9 1.4 %fusion.19 = bf16[224,192]{0,1:T(8,128)(2,1)S(1)} fusion(bf16[192,192]{1,0:T(8,128)(2,1)} %param.25, bf16[224,192]{1,0:T(8,128)(2,1)S(1)} %bitcast.84, bf16[192,192]{1,0:T(8,128)(2,1)} %param.23, f32[192]{0:T(256)} %param.24), kind=kOutput, calls=%fused_computation.19 | convolution fusion | flops 33202176 | bytes 320256 | tf_op jit(solution)/shard_map/dot_general | solution.py:104
  85.3 1.6 %fusion.43 = (f32[224]{0:T(256)S(1)}, f32[224,1792]{1,0:T(8,128)S(1)}) fusion(bf16[224,192]{0,1:T(8,128)(2,1)S(1)} %fusion.19, bf16[1792,192]{0,1:T(8,128)(2,1)} %reshape.197), kind=kOutput, calls=%fused_computation.93 | convolution fusion | flops 154541856 | bytes 2380672 | tf_op jit(solution)/shard_map/fqc,fkc->fqk/dot_general | solution.py:62
  87.3 1.1 %fusion.17 = bf16[224,192]{0,1:T(8,128)(2,1)} fusion(bf16[1792,192]{0,1:T(8,128)(2,1)S(1)} %copy-done.1, f32[224,1792]{1,0:T(8,128)S(1)} %get-tuple-element.56, f32[224]{0:T(256)S(1)} %broadcast_maximum_fusion, f32[224]{0:T(256)S(1)} %fusion.4), kind=kOutput, calls=%fused_computation.17 | convolution fusion | flops 155029504 | bytes 2381568 | tf_op jit(solution)/shard_map/fqk,fkc->fqc/dot_general | solution.py:66
  88.4 1.4 %fusion.15 = f32[224,192]{0,1:T(8,128)S(1)} fusion(f32[224,192]{0,1:T(8,128)S(1)} %copy-done.2, bf16[192,192]{1,0:T(8,128)(2,1)} %param.28, bf16[224,192]{0,1:T(8,128)(2,1)} %fusion.17, bf16[192,192]{1,0:T(8,128)(2,1)} %param.26, f32[192]{0:T(256)S(1)} %copy-done.5, f32[192]{0:T(256)S(1)} %copy-done.6), kind=kOutput, calls=%fused_computation.12 | convolution fusion | flops 33202176 | bytes 579072 | tf_op jit(solution)/shard_map/dot_general | solution.py:131
  (49 shorter events, 5.4 us)
Async XLA Ops:
  0.0 22.2 %copy-start = (bf16[3,3,3,192,192]{4,3,2,1,0:T(8,128)(2,1)S(1)}, bf16[3,3,3,192,192]{4,3,2,1,0:T(8,128)(2,1)}, u32[]{:S(2)}) copy-start(bf16[3,3,3,192,192]{4,3,2,1,0:T(8,128)(2,1)} %param.17) | copy-start | bytes 5971972
  2.1 1.5 %collective-permute-start = (bf16[1,2,112,192]{3,2,1,0:T(8,128)(2,1)S(1)}, bf16[1,2,112,192]{3,2,1,0:T(8,128)(2,1)S(1)}, u32[]{:S(2)}, u32[]{:S(2)}) collective-permute-start(bf16[1,2,112,192]{3,2,1,0:T(8,128)(2,1)S(1)} %fusion.31), channel_id=1, source_target_pairs={{1,0},{0,1},{3,2},{2,3},{5,4},{4,5},{7,6},{6,7},{9,8},{8,9},{11,10... | collective-permute-start | bytes 258056 | tf_op jit(solution)/shard_map/ppermute | solution.py:13
  3.7 7.5 %collective-permute-start.1 = (bf16[2,1,1,112,192]{4,3,2,1,0:T(8,128)(2,1)S(1)}, bf16[2,1,1,112,192]{4,3,2,1,0:T(8,128)(2,1)S(1)}, u32[]{:S(2)}, u32[]{:S(2)}) collective-permute-start(bf16[2,1,1,112,192]{4,3,2,1,0:T(8,128)(2,1)S(1)} %get-tuple-element.47), channel_id=1, source_target_pairs={{0,2},{2,4},{4,6},{6,8},{8,10},{10,12},{12,14},{1,3},{3,5},{5,7},{... | collective-permute-start | bytes 258056 | tf_op jit(solution)/shard_map/ppermute | solution.py:23
  8.4 6.8 %collective-permute-start.2 = (bf16[2,1,1,112,192]{4,3,2,1,0:T(8,128)(2,1)S(1)}, bf16[2,1,1,112,192]{4,3,2,1,0:T(8,128)(2,1)S(1)}, u32[]{:S(2)}, u32[]{:S(2)}) collective-permute-start(bf16[2,1,1,112,192]{4,3,2,1,0:T(8,128)(2,1)S(1)} %get-tuple-element.48), channel_id=1, source_target_pairs={{2,0},{4,2},{6,4},{8,6},{10,8},{12,10},{14,12},{3,1},{5,3},{7,5},{... | collective-permute-start | bytes 258056 | tf_op jit(solution)/shard_map/ppermute | solution.py:24
  16.8 5.4 %copy-start.7 = (f32[192]{0:T(256)S(1)}, f32[192]{0:T(256)}, u32[]{:S(2)}) copy-start(f32[192]{0:T(256)} %param.18) | copy-start | bytes 2308
  22.3 2.6 %copy-start.3 = (f32[192]{0:T(256)S(1)}, f32[192]{0:T(256)}, u32[]{:S(2)}) copy-start(f32[192]{0:T(256)} %param.19) | copy-start | bytes 2308
  25.0 1.4 %collective-permute-start.3 = (bf16[1,2,112,192]{3,2,1,0:T(8,128)(2,1)S(1)}, bf16[1,2,112,192]{3,2,1,0:T(8,128)(2,1)S(1)}, u32[]{:S(2)}, u32[]{:S(2)}) collective-permute-start(bf16[1,2,112,192]{3,2,1,0:T(8,128)(2,1)S(1)} %fusion.55), channel_id=1, source_target_pairs={{1,0},{0,1},{3,2},{2,3},{5,4},{4,5},{7,6},{6,7},{9,8},{8,9},{11,10... | collective-permute-start | bytes 258056 | tf_op jit(solution)/shard_map/ppermute | solution.py:13
  26.4 7.1 %collective-permute-start.4 = (bf16[2,1,1,112,192]{4,3,2,1,0:T(8,128)(2,1)S(1)}, bf16[2,1,1,112,192]{4,3,2,1,0:T(8,128)(2,1)S(1)}, u32[]{:S(2)}, u32[]{:S(2)}) collective-permute-start(bf16[2,1,1,112,192]{4,3,2,1,0:T(8,128)(2,1)S(1)} %get-tuple-element.27), channel_id=1, source_target_pairs={{0,2},{2,4},{4,6},{6,8},{8,10},{10,12},{12,14},{1,3},{3,5},{5,7},{... | collective-permute-start | bytes 258056 | tf_op jit(solution)/shard_map/ppermute | solution.py:23
  30.8 6.8 %collective-permute-start.5 = (bf16[2,1,1,112,192]{4,3,2,1,0:T(8,128)(2,1)S(1)}, bf16[2,1,1,112,192]{4,3,2,1,0:T(8,128)(2,1)S(1)}, u32[]{:S(2)}, u32[]{:S(2)}) collective-permute-start(bf16[2,1,1,112,192]{4,3,2,1,0:T(8,128)(2,1)S(1)} %get-tuple-element.28), channel_id=1, source_target_pairs={{2,0},{4,2},{6,4},{8,6},{10,8},{12,10},{14,12},{3,1},{5,3},{7,5},{... | collective-permute-start | bytes 258056 | tf_op jit(solution)/shard_map/ppermute | solution.py:24
  39.7 5.4 %copy-start.8 = (f32[192]{0:T(256)S(1)}, f32[192]{0:T(256)}, u32[]{:S(2)}) copy-start(f32[192]{0:T(256)} %param.21) | copy-start | bytes 2308
  45.1 3.4 %copy-start.4 = (f32[192]{0:T(256)S(1)}, f32[192]{0:T(256)}, u32[]{:S(2)}) copy-start(f32[192]{0:T(256)} %param.22) | copy-start | bytes 2308
  83.8 3.4 %copy-start.1 = (bf16[1792,192]{0,1:T(8,128)(2,1)S(1)}, bf16[1792,192]{0,1:T(8,128)(2,1)}, u32[]{:S(2)}) copy-start(bf16[1792,192]{0,1:T(8,128)(2,1)} %reshape.197) | copy-start | bytes 2064388
  86.9 1.6 %copy-start.2 = (f32[224,192]{0,1:T(8,128)S(1)}, f32[224,192]{0,1:T(8,128)}, u32[]{:S(2)}) copy-start(f32[224,192]{0,1:T(8,128)} %copy.38) | copy-start | bytes 516100
  86.9 1.6 %copy-start.5 = (f32[192]{0:T(256)S(1)}, f32[192]{0:T(256)}, u32[]{:S(2)}) copy-start(f32[192]{0:T(256)} %param.29) | copy-start | bytes 2308
  86.9 1.5 %copy-start.6 = (f32[192]{0:T(256)S(1)}, f32[192]{0:T(256)}, u32[]{:S(2)}) copy-start(f32[192]{0:T(256)} %param.27) | copy-start | bytes 2308
where the time goes:
time: 91.8 us; the launch traced here: 90.7 us
  blocking collectives  32.1 us (35%)
  local copies, waits for them, and re-layouts  19.6 us (21%)
  starting transfers between devices  12.3 us (13%)
  waiting for transfers between devices  12.2 us (13%)
  matrix products  11.4 us (12%)
  other arithmetic  2.82 us (3%)
    all_gather x1, blocking collectives, local(): lax.all_gather(normed[0], 'space', axis=0, tiled=True)  32.1 us
    concatenate x2, local copies, waits for them, and re-layouts, causal_conv(): jnp.concatenate(tap_list, axis=-1)  10.8 us
    ppermute x2, starting transfers between devices, extended(): before = lax.ppermute(last, axis, up)  9.11 us
    ppermute x2, waiting for transfers between devices, extended(): after = lax.ppermute(first, axis, down)  8.24 us
    dot_general x2, matrix products, causal_conv(): jnp.dot(patches, weight.reshape(27 * channels, channels), preferred_eleme...  5.88 us
    slice x5, local copies, waits for them, and re-layouts, causal_conv(): widened[:, row_off:row_off + row_count, col_off:col_off + col_count, :]  3.21 us
    ppermute x2, waiting for transfers between devices, extended(): before = lax.ppermute(last, axis, up)  2.7 us
    ppermute x2, starting transfers between devices, extended(): after = lax.ppermute(first, axis, down)  2.58 us
  transfers between devices with their start and end apart: 6, of which 6 were waited for; matrix products, arithmetic and copies ran while one was open for 1% of the time, Pallas kernels for 0%

commit v1 on v0

--- a/solution.py
+++ b/solution.py
@@ -3,6 +3,7 @@
 import jax.numpy as jnp
 from jax import lax
 from jax.sharding import PartitionSpec as P
+from jax.lax import axis_index, ppermute, psum
 
 epsilon = 1e-06
 
@@ -86,6 +87,25 @@
     w_out,
     b_out,
 ):
+
+    def change_view(own_rows, across):
+        passed, top, m_next = (psum(1, across), axis_index(across), own_rows.shape[0])
+        w_next = jnp.zeros(
+            [i0 * passed if idx == 0 else i0 for idx, i0 in enumerate(own_rows.shape)],
+            own_rows.dtype,
+        )
+        left_arr = lax.dynamic_update_slice_in_dim(w_next, own_rows, top * m_next, axis=0)
+        pp = 1
+        while pp < passed:
+            own_rows = ppermute(
+                own_rows, across, [(idx, (idx + 1) % passed) for idx in range(passed)]
+            )
+            left_arr = lax.dynamic_update_slice_in_dim(
+                left_arr, own_rows, (top - pp) % passed * m_next, axis=0
+            )
+            pp = pp + 1
+        return left_arr
+
     local_frames = frames[:, 0]
     frame_count, row_count, col_count, channels = local_frames.shape
     frame_values = local_frames.astype(jnp.float32)
@@ -115,11 +135,7 @@
         return absorb(running, slot_queries, received.reshape(1, -1, channels))
 
     start_state = tuple((item for item in initial))
-    results = [
-        absorb_one(
-            start_state, lax.all_gather(normed[0], "space", axis=0, tiled=True), jnp.int32(0)
-        )
-    ]
+    results = [absorb_one(start_state, change_view(normed[0], "space"), jnp.int32(0))]
     total = jnp.concatenate([item[1] for item in results], axis=0)
     accum = jnp.concatenate([item[2] for item in results], axis=0)
     mixed = (accum / total[..., None]).astype(jnp.bfloat16).reshape(-1, channels)

time: 91.8 us -> 116 us (1.26)
  waiting for transfers between devices: 12.2 us -> 60.4 us
  blocking collectives: 32.1 us -> 0 us
  other arithmetic: 2.82 us -> 6.51 us
  local copies, waits for them, and re-layouts: 19.6 us -> 22 us
  starting transfers between devices: 12.3 us -> 14 us
    ppermute x0 -> x7, waiting for transfers between devices: none -> 47.9 us  [change_view(): ppermute(own_rows, across, [(idx, (idx + 1) % passed) for idx in range(pa...]
    all_gather x1 -> x0, blocking collectives: 32.1 us -> none  [local(): lax.all_gather(normed[0], 'space', axis=0, tiled=True)]
    dynamic_update_slice x0 -> x7, local copies, waits for them, and re-layouts: none -> 4.53 us  [change_view(): lax.dynamic_update_slice_in_dim(left_arr, own_rows, (top - pp) % passed *...]
    another operation x1 -> x0, local copies, waits for them, and re-layouts: 1.81 us -> none
    ppermute x0 -> x7, starting transfers between devices: none -> 1.73 us  [change_view(): ppermute(own_rows, across, [(idx, (idx + 1) % passed) for idx in range(pa...]
    reduce_sum x1, other arithmetic: 0.37 us -> 1.82 us  [absorb(): total_new = jnp.sum(weights, axis=-1)]
    dot_general x1, matrix products: 1.59 us -> 2.94 us  [absorb(): jnp.einsum('fqc,fkc->fqk', queries, key_rows, preferred_element_type=jnp....]
    dot_general x1, matrix products: 1.4 us -> 0.17 us  [local(): jnp.dot(flat, w_query, preferred_element_type=jnp.float32) + b_query]
  transfers between devices with their start and end apart: 6 -> 13, of which waited for: 6 -> 13; matrix products, arithmetic and copies ran while one was open for 1% -> 5% of each run, Pallas kernels for 0% -> 0%
where the time goes in v1:
time: 116 us; the launch traced here: 115 us
  waiting for transfers between devices  60.4 us (52%)
  local copies, waits for them, and re-layouts  22 us (19%)
  starting transfers between devices  14 us (12%)
  matrix products  11.5 us (10%)
  other arithmetic  6.51 us (6%)
    ppermute x7, waiting for transfers between devices, change_view(): ppermute(own_rows, across, [(idx, (idx + 1) % passed) for idx in range(pa...  47.9 us
    concatenate x2, local copies, waits for them, and re-layouts, causal_conv(): jnp.concatenate(tap_list, axis=-1)  10.9 us
    ppermute x2, starting transfers between devices, extended(): before = lax.ppermute(last, axis, up)  9.1 us
    ppermute x2, waiting for transfers between devices, extended(): after = lax.ppermute(first, axis, down)  8.24 us
    dot_general x2, matrix products, causal_conv(): jnp.dot(patches, weight.reshape(27 * channels, channels), preferred_eleme...  5.92 us
    dynamic_update_slice x7, local copies, waits for them, and re-layouts, change_view(): lax.dynamic_update_slice_in_dim(left_arr, own_rows, (top - pp) % passed *...  4.53 us
    slice x5, local copies, waits for them, and re-layouts, causal_conv(): widened[:, row_off:row_off + row_count, col_off:col_off + col_count, :]  3.19 us
    dot_general x1, matrix products, absorb(): jnp.einsum('fqc,fkc->fqk', queries, key_rows, preferred_element_type=jnp....  2.94 us
  transfers between devices with their start and end apart: 13, of which 13 were waited for; matrix products, arithmetic and copies ran while one was open for 5% of the time, Pallas kernels for 0%

profile of v1, /device:TPU:0, one launch (start us, length us, event | category | flops | bytes accessed | tf_op | source)
XLA Modules:
  0.0 114.9 jit_solution(10368369135242089654)
XLA Ops:
  3.7 4.8 %collective-permute-start.1 = (bf16[2,1,1,112,192]{4,3,2,1,0:T(8,128)(2,1)S(1)}, bf16[2,1,1,112,192]{4,3,2,1,0:T(8,128)(2,1)S(1)}, u32[]{:S(2)}, u32[]{:S(2)}) collective-permute-start(bf16[2,1,1,112,192]{4,3,2,1,0:T(8,128)(2,1)S(1)} %get-tuple-element.49), channel_id=1, source_target_pairs={{0,2},{2,4},{4,6},{6,8},{8,10},{10,12},{12,14},{1,3},{3,5},{5,7},{... | collective-permute-start | bytes 258056 | tf_op jit(solution)/shard_map/ppermute | solution.py:24
  8.4 1.3 %collective-permute-start.2 = (bf16[2,1,1,112,192]{4,3,2,1,0:T(8,128)(2,1)S(1)}, bf16[2,1,1,112,192]{4,3,2,1,0:T(8,128)(2,1)S(1)}, u32[]{:S(2)}, u32[]{:S(2)}) collective-permute-start(bf16[2,1,1,112,192]{4,3,2,1,0:T(8,128)(2,1)S(1)} %get-tuple-element.50), channel_id=1, source_target_pairs={{2,0},{4,2},{6,4},{8,6},{10,8},{12,10},{14,12},{3,1},{5,3},{7,5},{... | collective-permute-start | bytes 258056 | tf_op jit(solution)/shard_map/ppermute | solution.py:25
  9.8 1.3 %collective-permute-done.1 = bf16[2,1,1,112,192]{4,3,2,1,0:T(8,128)(2,1)S(1)} collective-permute-done((bf16[2,1,1,112,192]{4,3,2,1,0:T(8,128)(2,1)S(1)}, bf16[2,1,1,112,192]{4,3,2,1,0:T(8,128)(2,1)S(1)}, u32[]{:S(2)}, u32[]{:S(2)}) %collective-permute-start.1) | collective-permute-done | bytes 86048 | tf_op jit(solution)/shard_map/ppermute | solution.py:24
  11.1 4.1 %collective-permute-done.2 = bf16[2,1,1,112,192]{4,3,2,1,0:T(8,128)(2,1)S(1)} collective-permute-done((bf16[2,1,1,112,192]{4,3,2,1,0:T(8,128)(2,1)S(1)}, bf16[2,1,1,112,192]{4,3,2,1,0:T(8,128)(2,1)S(1)}, u32[]{:S(2)}, u32[]{:S(2)}) %collective-permute-start.2) | collective-permute-done | bytes 86048 | tf_op jit(solution)/shard_map/ppermute | solution.py:25
  15.4 1.2 %pad_slice_fusion.16 = (bf16[1,2,112,192]{3,2,1,0:T(8,128)(2,1)S(1)}, bf16[1,2,112,192]{3,2,1,0:T(8,128)(2,1)S(1)}, bf16[1,2,112,192]{3,2,1,0:T(8,128)(2,1)S(1)}...) fusion(bf16[1,4,112,192]{3,2,1,0:T(8,128)(2,1)S(1)} %get-tuple-, ...), kind=kLoop, calls=%fused_computation.68 | loop fusion | bytes 2695168 | tf_op jit(solution)/shard_map/slice | solution.py:50
  16.8 5.4 %concatenate.13 = bf16[1,2,112,5184]{3,2,1,0:T(8,128)(2,1)} concatenate(bf16[1,2,112,192]{3,2,1,0:T(8,128)(2,1)S(1)} %pad.24, bf16[1,2,112,192]{3,2,1,0:T(8,128)(2,1)S(1)} %pad.25, bf16[1,2,112,192]{3,2,1,0:T(8,128)(2,1)S(1)} %pad.26, bf16[1,2,112,192]{3,2,1,0:T(8,128)(2,1)S(1)} %pad.24, bf16[1,2,112,192]{3,2,1,0:T(8,128)(2,1)S(1)} %pad.25, bf16[1,2,112,192]{3,2,1,0:T(8,128)(2,1)S(1)} %pad.26, ...), dimensions={3} | concatenate | bytes 4644864 | tf_op jit(solution)/shard_map/concatenate | solution.py:52
  22.3 2.5 %multiply_reduce_fusion.1 = (f32[2,112]{1,0:T(2,128)S(1)}, f32[2,112,192]{2,1,0:T(8,128)S(1)}) fusion(f32[192]{0:T(256)S(1)} %copy-done.10, bf16[5184,192,1]{1,0,2:T(8,128)(2,1)S(1)} %bitcast.82, bf16[1,2,112,5184]{3,2,1,0:T(8,128)(2,1)} %concatenate.13), kind=kOutput, calls=%fused_computation.55 | convolution fusion | flops 446035744 | bytes 4486784 | tf_op jit(solution)/shard_map/dot_general | solution.py:55
  27.1 4.3 %collective-permute-start.4 = (bf16[2,1,1,112,192]{4,3,2,1,0:T(8,128)(2,1)}, bf16[2,1,1,112,192]{4,3,2,1,0:T(8,128)(2,1)S(1)}, u32[]{:S(2)}, u32[]{:S(2)}) collective-permute-start(bf16[2,1,1,112,192]{4,3,2,1,0:T(8,128)(2,1)} %get-tuple-element.29), channel_id=1, source_target_pairs={{0,2},{2,4},{4,6},{6,8},{8,10},{10,12},{12,14},{1,3},{3,5},{5,7},{... | collective-permute-start | bytes 258056 | tf_op jit(solution)/shard_map/ppermute | solution.py:24
  31.5 1.3 %collective-permute-start.5 = (bf16[2,1,1,112,192]{4,3,2,1,0:T(8,128)(2,1)}, bf16[2,1,1,112,192]{4,3,2,1,0:T(8,128)(2,1)}, u32[]{:S(2)}, u32[]{:S(2)}) collective-permute-start(bf16[2,1,1,112,192]{4,3,2,1,0:T(8,128)(2,1)} %get-tuple-element.30), channel_id=1, source_target_pairs={{2,0},{4,2},{6,4},{8,6},{10,8},{12,10},{14,12},{3,1},{5,3},{7,5},{... | collective-permute-start | bytes 258056 | tf_op jit(solution)/shard_map/ppermute | solution.py:25
  32.9 1.6 %collective-permute-done.4 = bf16[2,1,1,112,192]{4,3,2,1,0:T(8,128)(2,1)S(1)} collective-permute-done((bf16[2,1,1,112,192]{4,3,2,1,0:T(8,128)(2,1)}, bf16[2,1,1,112,192]{4,3,2,1,0:T(8,128)(2,1)S(1)}, u32[]{:S(2)}, u32[]{:S(2)}) %collective-permute-start.4) | collective-permute-done | bytes 86048 | tf_op jit(solution)/shard_map/ppermute | solution.py:24
  34.5 4.1 %collective-permute-done.5 = bf16[2,1,1,112,192]{4,3,2,1,0:T(8,128)(2,1)} collective-permute-done((bf16[2,1,1,112,192]{4,3,2,1,0:T(8,128)(2,1)}, bf16[2,1,1,112,192]{4,3,2,1,0:T(8,128)(2,1)}, u32[]{:S(2)}, u32[]{:S(2)}) %collective-permute-start.5) | collective-permute-done | bytes 86048 | tf_op jit(solution)/shard_map/ppermute | solution.py:25
  41.5 5.4 %concatenate.15 = bf16[1,2,112,5184]{3,2,1,0:T(8,128)(2,1)} concatenate(bf16[1,2,112,192]{3,2,1,0:T(8,128)(2,1)S(1)} %pad.24, bf16[1,2,112,192]{3,2,1,0:T(8,128)(2,1)S(1)} %pad.25, bf16[1,2,112,192]{3,2,1,0:T(8,128)(2,1)S(1)} %pad.26, bf16[1,2,112,192]{3,2,1,0:T(8,128)(2,1)S(1)} %pad.24, bf16[1,2,112,192]{3,2,1,0:T(8,128)(2,1)S(1)} %pad.25, bf16[1,2,112,192]{3,2,1,0:T(8,128)(2,1)S(1)} %pad.26, ...), dimensions={3} | concatenate | bytes 4644864 | tf_op jit(solution)/shard_map/concatenate | solution.py:52
  47.0 3.4 %multiply_reduce_fusion = (f32[2,112]{1,0:T(2,128)S(1)}, f32[2,112,192]{2,1,0:T(8,128)S(1)}) fusion(f32[192]{0:T(256)S(1)} %copy-done.11, bf16[5184,192,1]{1,0,2:T(8,128)(2,1)} %bitcast.85, bf16[1,2,112,5184]{3,2,1,0:T(8,128)(2,1)} %concatenate.15, bf16[1,1,2,112,192]{4,3,2,1,0:T(8,128)(2,1)S(1)} %copy.16), kind=kOutput, calls=%fused_computation.53 | convolution fusion | flops 446121760 | bytes 4572800 | tf_op jit(solution)/shard_map/dot_general | solution.py:55
  52.2 1.7 %collective-permute-start.6 = (bf16[2,112,192]{2,1,0:T(8,128)(2,1)S(1)}, bf16[2,112,192]{2,1,0:T(8,128)(2,1)S(1)}, u32[]{:S(2)}, u32[]{:S(2)}) collective-permute-start(bf16[2,112,192]{2,1,0:T(8,128)(2,1)S(1)} %get-tuple-element.6), channel_id=1, source_target_pairs={{0,2},{2,4},{4,6},{6,8},{8,10},{10,12},{12,14},{14,0},{1,3},{3,5},... | collective-permute-start | bytes 258056 | tf_op jit(solution)/shard_map/ppermute | solution.py:100
  54.2 5.5 %collective-permute-done.6 = bf16[2,112,192]{2,1,0:T(8,128)(2,1)S(1)} collective-permute-done((bf16[2,112,192]{2,1,0:T(8,128)(2,1)S(1)}, bf16[2,112,192]{2,1,0:T(8,128)(2,1)S(1)}, u32[]{:S(2)}, u32[]{:S(2)}) %collective-permute-start.6) | collective-permute-done | bytes 86048 | tf_op jit(solution)/shard_map/ppermute | solution.py:100
  60.3 6.8 %collective-permute-done.7 = bf16[2,112,192]{2,1,0:T(8,128)(2,1)S(1)} collective-permute-done((bf16[2,112,192]{2,1,0:T(8,128)(2,1)S(1)}, bf16[2,112,192]{2,1,0:T(8,128)(2,1)S(1)}, u32[]{:S(2)}, u32[]{:S(2)}) %collective-permute-start.7) | collective-permute-done | bytes 86048 | tf_op jit(solution)/shard_map/ppermute | solution.py:100
  67.8 6.8 %collective-permute-done.8 = bf16[2,112,192]{2,1,0:T(8,128)(2,1)S(1)} collective-permute-done((bf16[2,112,192]{2,1,0:T(8,128)(2,1)S(1)}, bf16[2,112,192]{2,1,0:T(8,128)(2,1)S(1)}, u32[]{:S(2)}, u32[]{:S(2)}) %collective-permute-start.8) | collective-permute-done | bytes 86048 | tf_op jit(solution)/shard_map/ppermute | solution.py:100
  75.3 7.2 %collective-permute-done.9 = bf16[2,112,192]{2,1,0:T(8,128)(2,1)S(1)} collective-permute-done((bf16[2,112,192]{2,1,0:T(8,128)(2,1)S(1)}, bf16[2,112,192]{2,1,0:T(8,128)(2,1)S(1)}, u32[]{:S(2)}, u32[]{:S(2)}) %collective-permute-start.9) | collective-permute-done | bytes 86048 | tf_op jit(solution)/shard_map/ppermute | solution.py:100
  83.1 7.8 %collective-permute-done.10 = bf16[2,112,192]{2,1,0:T(8,128)(2,1)S(1)} collective-permute-done((bf16[2,112,192]{2,1,0:T(8,128)(2,1)S(1)}, bf16[2,112,192]{2,1,0:T(8,128)(2,1)S(1)}, u32[]{:S(2)}, u32[]{:S(2)}) %collective-permute-start.10) | collective-permute-done | bytes 86048 | tf_op jit(solution)/shard_map/ppermute | solution.py:100
  91.6 7.0 %collective-permute-done.11 = bf16[2,112,192]{2,1,0:T(8,128)(2,1)S(1)} collective-permute-done((bf16[2,112,192]{2,1,0:T(8,128)(2,1)S(1)}, bf16[2,112,192]{2,1,0:T(8,128)(2,1)S(1)}, u32[]{:S(2)}, u32[]{:S(2)}) %collective-permute-start.11) | collective-permute-done | bytes 86048 | tf_op jit(solution)/shard_map/ppermute | solution.py:100
  99.2 6.8 %collective-permute-done.12 = bf16[2,112,192]{2,1,0:T(8,128)(2,1)S(1)} collective-permute-done((bf16[2,112,192]{2,1,0:T(8,128)(2,1)S(1)}, bf16[2,112,192]{2,1,0:T(8,128)(2,1)S(1)}, u32[]{:S(2)}, u32[]{:S(2)}) %collective-permute-start.12) | collective-permute-done | bytes 86048 | tf_op jit(solution)/shard_map/ppermute | solution.py:100
  106.7 2.9 %fusion.45 = (f32[224]{0:T(256)S(1)}, f32[224,1792]{1,0:T(8,128)}) fusion(bf16[1792,192]{1,0:T(8,128)(2,1)} %bitcast.18, bf16[224,192]{1,0:T(8,128)(2,1)S(1)} %fusion.16, bf16[192,192]{1,0:T(8,128)(2,1)S(1)} %copy-done.1), kind=kOutput, calls=%fused_computation.103 | convolution fusion | flops 171142944 | bytes 2454400 | tf_op jit(solution)/shard_map/fqc,fkc->fqk/dot_general | solution.py:63
  109.7 1.8 %fusion.4 = f32[224]{0:T(256)S(1)} fusion(f32[224,1792]{1,0:T(8,128)} %get-tuple-element.58, f32[224]{0:T(256)S(1)} %broadcast_maximum_fusion), kind=kLoop, calls=%fused_computation.5 | loop fusion | flops 802592 | bytes 1607424 | tf_op jit(solution)/shard_map/reduce_sum | solution.py:66
  111.5 2.1 %fusion.18 = bf16[224,192]{1,0:T(8,128)(2,1)S(1)} fusion(bf16[1792,192]{1,0:T(8,128)(2,1)} %bitcast.18, f32[224,1792]{1,0:T(8,128)} %get-tuple-element.58, f32[224]{0:T(256)S(1)} %broadcast_maximum_fusion, f32[224]{0:T(256)S(1)} %fusion.4), kind=kOutput, calls=%fused_computation.18 | convolution fusion | flops 155029504 | bytes 2381568 | tf_op jit(solution)/shard_map/fqk,fkc->fqc/dot_general | solution.py:67
  (73 shorter events, 17.1 us)
Async XLA Ops:
  0.0 22.2 %copy-start = (bf16[3,3,3,192,192]{4,3,2,1,0:T(8,128)(2,1)S(1)}, bf16[3,3,3,192,192]{4,3,2,1,0:T(8,128)(2,1)}, u32[]{:S(2)}) copy-start(bf16[3,3,3,192,192]{4,3,2,1,0:T(8,128)(2,1)} %param.17) | copy-start | bytes 5971972
  2.1 1.5 %collective-permute-start = (bf16[1,2,112,192]{3,2,1,0:T(8,128)(2,1)S(1)}, bf16[1,2,112,192]{3,2,1,0:T(8,128)(2,1)S(1)}, u32[]{:S(2)}, u32[]{:S(2)}) collective-permute-start(bf16[1,2,112,192]{3,2,1,0:T(8,128)(2,1)S(1)} %fusion.32), channel_id=1, source_target_pairs={{1,0},{0,1},{3,2},{2,3},{5,4},{4,5},{7,6},{6,7},{9,8},{8,9},{11,10... | collective-permute-start | bytes 258056 | tf_op jit(solution)/shard_map/ppermute | solution.py:14
  3.7 7.5 %collective-permute-start.1 = (bf16[2,1,1,112,192]{4,3,2,1,0:T(8,128)(2,1)S(1)}, bf16[2,1,1,112,192]{4,3,2,1,0:T(8,128)(2,1)S(1)}, u32[]{:S(2)}, u32[]{:S(2)}) collective-permute-start(bf16[2,1,1,112,192]{4,3,2,1,0:T(8,128)(2,1)S(1)} %get-tuple-element.49), channel_id=1, source_target_pairs={{0,2},{2,4},{4,6},{6,8},{8,10},{10,12},{12,14},{1,3},{3,5},{5,7},{... | collective-permute-start | bytes 258056 | tf_op jit(solution)/shard_map/ppermute | solution.py:24
  8.4 6.8 %collective-permute-start.2 = (bf16[2,1,1,112,192]{4,3,2,1,0:T(8,128)(2,1)S(1)}, bf16[2,1,1,112,192]{4,3,2,1,0:T(8,128)(2,1)S(1)}, u32[]{:S(2)}, u32[]{:S(2)}) collective-permute-start(bf16[2,1,1,112,192]{4,3,2,1,0:T(8,128)(2,1)S(1)} %get-tuple-element.50), channel_id=1, source_target_pairs={{2,0},{4,2},{6,4},{8,6},{10,8},{12,10},{14,12},{3,1},{5,3},{7,5},{... | collective-permute-start | bytes 258056 | tf_op jit(solution)/shard_map/ppermute | solution.py:25
  16.8 5.5 %copy-start.10 = (f32[192]{0:T(256)S(1)}, f32[192]{0:T(256)}, u32[]{:S(2)}) copy-start(f32[192]{0:T(256)} %param.18) | copy-start | bytes 2308
  25.0 1.4 %collective-permute-start.3 = (bf16[1,2,112,192]{3,2,1,0:T(8,128)(2,1)S(1)}, bf16[1,2,112,192]{3,2,1,0:T(8,128)(2,1)S(1)}, u32[]{:S(2)}, u32[]{:S(2)}) collective-permute-start(bf16[1,2,112,192]{3,2,1,0:T(8,128)(2,1)S(1)} %fusion.57), channel_id=1, source_target_pairs={{1,0},{0,1},{3,2},{2,3},{5,4},{4,5},{7,6},{6,7},{9,8},{8,9},{11,10... | collective-permute-start | bytes 258056 | tf_op jit(solution)/shard_map/ppermute | solution.py:14
  27.1 7.4 %collective-permute-start.4 = (bf16[2,1,1,112,192]{4,3,2,1,0:T(8,128)(2,1)}, bf16[2,1,1,112,192]{4,3,2,1,0:T(8,128)(2,1)S(1)}, u32[]{:S(2)}, u32[]{:S(2)}) collective-permute-start(bf16[2,1,1,112,192]{4,3,2,1,0:T(8,128)(2,1)} %get-tuple-element.29), channel_id=1, source_target_pairs={{0,2},{2,4},{4,6},{6,8},{8,10},{10,12},{12,14},{1,3},{3,5},{5,7},{... | collective-permute-start | bytes 258056 | tf_op jit(solution)/shard_map/ppermute | solution.py:24
  31.5 7.1 %collective-permute-start.5 = (bf16[2,1,1,112,192]{4,3,2,1,0:T(8,128)(2,1)}, bf16[2,1,1,112,192]{4,3,2,1,0:T(8,128)(2,1)}, u32[]{:S(2)}, u32[]{:S(2)}) collective-permute-start(bf16[2,1,1,112,192]{4,3,2,1,0:T(8,128)(2,1)} %get-tuple-element.30), channel_id=1, source_target_pairs={{2,0},{4,2},{6,4},{8,6},{10,8},{12,10},{14,12},{3,1},{5,3},{7,5},{... | collective-permute-start | bytes 258056 | tf_op jit(solution)/shard_map/ppermute | solution.py:25
  41.5 5.4 %copy-start.11 = (f32[192]{0:T(256)S(1)}, f32[192]{0:T(256)}, u32[]{:S(2)}) copy-start(f32[192]{0:T(256)} %param.21) | copy-start | bytes 2308
  47.0 4.5 %copy-start.6 = (f32[192]{0:T(256)S(1)}, f32[192]{0:T(256)}, u32[]{:S(2)}) copy-start(f32[192]{0:T(256)} %param.22) | copy-start | bytes 2308
  47.0 6.9 %copy-start.2 = (bf16[192,192]{1,0:T(8,128)(2,1)S(1)}, bf16[192,192]{1,0:T(8,128)(2,1)}, u32[]{:S(2)}) copy-start(bf16[192,192]{1,0:T(8,128)(2,1)} %param.23) | copy-start | bytes 221188
  47.0 6.9 %copy-start.7 = (f32[192]{0:T(256)S(1)}, f32[192]{0:T(256)}, u32[]{:S(2)}) copy-start(f32[192]{0:T(256)} %param.24) | copy-start | bytes 2308
  50.4 56.3 %copy-start.1 = (bf16[192,192]{1,0:T(8,128)(2,1)S(1)}, bf16[192,192]{1,0:T(8,128)(2,1)}, u32[]{:S(2)}) copy-start(bf16[192,192]{1,0:T(8,128)(2,1)} %param.25) | copy-start | bytes 221188
  52.2 7.5 %collective-permute-start.6 = (bf16[2,112,192]{2,1,0:T(8,128)(2,1)S(1)}, bf16[2,112,192]{2,1,0:T(8,128)(2,1)S(1)}, u32[]{:S(2)}, u32[]{:S(2)}) collective-permute-start(bf16[2,112,192]{2,1,0:T(8,128)(2,1)S(1)} %get-tuple-element.6), channel_id=1, source_target_pairs={{0,2},{2,4},{4,6},{6,8},{8,10},{10,12},{12,14},{14,0},{1,3},{3,5},... | collective-permute-start | bytes 258056 | tf_op jit(solution)/shard_map/ppermute | solution.py:100
  59.7 7.5 %collective-permute-start.7 = (bf16[2,112,192]{2,1,0:T(8,128)(2,1)S(1)}, bf16[2,112,192]{2,1,0:T(8,128)(2,1)S(1)}, u32[]{:S(2)}, u32[]{:S(2)}) collective-permute-start(bf16[2,112,192]{2,1,0:T(8,128)(2,1)S(1)} %collective-permute-done.6), channel_id=1, source_target_pairs={{0,2},{2,4},{4,6},{6,8},{8,10},{10,12},{12,14},{14,0},{1,3},{3,5},... | collective-permute-start | bytes 258056 | tf_op jit(solution)/shard_map/ppermute | solution.py:100
  67.2 7.5 %collective-permute-start.8 = (bf16[2,112,192]{2,1,0:T(8,128)(2,1)S(1)}, bf16[2,112,192]{2,1,0:T(8,128)(2,1)S(1)}, u32[]{:S(2)}, u32[]{:S(2)}) collective-permute-start(bf16[2,112,192]{2,1,0:T(8,128)(2,1)S(1)} %collective-permute-done.7), channel_id=1, source_target_pairs={{0,2},{2,4},{4,6},{6,8},{8,10},{10,12},{12,14},{14,0},{1,3},{3,5},... | collective-permute-start | bytes 258056 | tf_op jit(solution)/shard_map/ppermute | solution.py:100
  74.7 7.8 %collective-permute-start.9 = (bf16[2,112,192]{2,1,0:T(8,128)(2,1)S(1)}, bf16[2,112,192]{2,1,0:T(8,128)(2,1)S(1)}, u32[]{:S(2)}, u32[]{:S(2)}) collective-permute-start(bf16[2,112,192]{2,1,0:T(8,128)(2,1)S(1)} %collective-permute-done.8), channel_id=1, source_target_pairs={{0,2},{2,4},{4,6},{6,8},{8,10},{10,12},{12,14},{14,0},{1,3},{3,5},... | collective-permute-start | bytes 258056 | tf_op jit(solution)/shard_map/ppermute | solution.py:100
  82.5 8.5 %collective-permute-start.10 = (bf16[2,112,192]{2,1,0:T(8,128)(2,1)S(1)}, bf16[2,112,192]{2,1,0:T(8,128)(2,1)S(1)}, u32[]{:S(2)}, u32[]{:S(2)}) collective-permute-start(bf16[2,112,192]{2,1,0:T(8,128)(2,1)S(1)} %collective-permute-done.9), channel_id=1, source_target_pairs={{0,2},{2,4},{4,6},{6,8},{8,10},{10,12},{12,14},{14,0},{1,3},{3,5},... | collective-permute-start | bytes 258056 | tf_op jit(solution)/shard_map/ppermute | solution.py:100
  90.9 7.6 %collective-permute-start.11 = (bf16[2,112,192]{2,1,0:T(8,128)(2,1)S(1)}, bf16[2,112,192]{2,1,0:T(8,128)(2,1)S(1)}, u32[]{:S(2)}, u32[]{:S(2)}) collective-permute-start(bf16[2,112,192]{2,1,0:T(8,128)(2,1)S(1)} %collective-permute-done.10), channel_id=1, source_target_pairs={{0,2},{2,4},{4,6},{6,8},{8,10},{10,12},{12,14},{14,0},{1,3},{3,5},... | collective-permute-start | bytes 258056 | tf_op jit(solution)/shard_map/ppermute | solution.py:100
  98.6 7.5 %collective-permute-start.12 = (bf16[2,112,192]{2,1,0:T(8,128)(2,1)S(1)}, bf16[2,112,192]{2,1,0:T(8,128)(2,1)S(1)}, u32[]{:S(2)}, u32[]{:S(2)}) collective-permute-start(bf16[2,112,192]{2,1,0:T(8,128)(2,1)S(1)} %collective-permute-done.11), channel_id=1, source_target_pairs={{0,2},{2,4},{4,6},{6,8},{8,10},{10,12},{12,14},{14,0},{1,3},{3,5},... | collective-permute-start | bytes 258056 | tf_op jit(solution)/shard_map/ppermute | solution.py:100
  109.7 3.9 %copy-start.3 = (bf16[192,192]{1,0:T(8,128)(2,1)S(1)}, bf16[192,192]{1,0:T(8,128)(2,1)}, u32[]{:S(2)}) copy-start(bf16[192,192]{1,0:T(8,128)(2,1)} %param.28) | copy-start | bytes 221188
  109.7 4.0 %copy-start.4 = (bf16[192,192]{1,0:T(8,128)(2,1)S(1)}, bf16[192,192]{1,0:T(8,128)(2,1)}, u32[]{:S(2)}) copy-start(bf16[192,192]{1,0:T(8,128)(2,1)} %param.26) | copy-start | bytes 221188
  109.7 4.0 %copy-start.8 = (f32[192]{0:T(256)S(1)}, f32[192]{0:T(256)}, u32[]{:S(2)}) copy-start(f32[192]{0:T(256)} %param.27) | copy-start | bytes 2308
  109.7 4.0 %copy-start.9 = (f32[192]{0:T(256)S(1)}, f32[192]{0:T(256)}, u32[]{:S(2)}) copy-start(f32[192]{0:T(256)} %param.29) | copy-start | bytes 2308
  (1 other events, 2.6 us)
